TPU v7x, 32 devices: a whole 2x2x4 slice. The times are simulated.
32 devices in a mesh: store: 4 (over x, core), blk: 2 (over y), batch: 4 (over z).
Axes of the slice: x: 2, y: 2, z: 4, core: 2. Of those that a mesh axis runs over, the one named last changes fastest.
Arguments:
- cands: bfloat16 [16, 256, 1024], P(('batch', 'store'), 'blk'), parts along dimension 0, may hold values from -6 to 6
- kv_store: bfloat16 [16, 512, 2, 1024], P('batch', ('blk', 'store')), parts along dimension 0, may hold values from -6 to 6
- proj_weight: bfloat16 [1024, 2, 1024], P(None, None, 'blk'), may hold values from -0.1875 to 0.1875
- norm_gain: float32 [1024], replicated, may hold values from 0.5 to 1.5
- users: int32 [16], P('batch'), parts along dimension 0, may hold values from 0 to 3, each once
- lengths: int32 [16], P('batch'), parts along dimension 0, may hold values from 128 to 512, as said below
Outputs:
- scored: bfloat16 [16, 256, 1024], P(('batch', 'store'), 'blk'), parts along dimension 0
There are 4 independent parts, one for each index of `batch`. A program takes and returns all parts, laid end to end along the dimension named above; an argument that names none is the same for every part. Nothing has to cross between parts.
Inputs may be any that keep to these rules, and one draw needn't show every extreme that they name: A permutation of the users. `lengths`: some user has all 512 events live.
All inputs are finite; a program needn't handle non-finite values.
Results may differ from a plain program's by a relative error of at most 0.014.
Values may be sent and summed in bfloat16 or wider, within the bound.
No kernel may reach another device: no remote copies, remote signals or barrier semaphores. Data moves between devices by JAX's collectives and lax.ppermute only.
A program may use at most 64 MiB of HBM per device.

v0:
```python
import jax
import jax.numpy as jnp
from jax import lax
from jax.sharding import PartitionSpec as P
from jax.experimental.layout import Layout, with_layout_constraint

D = 1024
HEADS = 8
HEAD_SIZE = D // HEADS


def attend(qheads, keys, values, count):
    inverse = HEAD_SIZE ** (-0.5)
    local_heads, rows, _ = qheads.shape
    total = keys.shape[1]
    block = min(total, 512)
    scale_count = count.astype(jnp.float32)

    def one_block(index, accum):
        start = index * block
        key_block = lax.dynamic_slice_in_dim(keys, start, block, 1)
        value_block = lax.dynamic_slice_in_dim(values, start, block, 1)
        scores = (
            jnp.einsum("hcd,hkd->hck", qheads, key_block, preferred_element_type=jnp.float32)
            * inverse
        )
        live = (start + jnp.arange(block) < count).astype(jnp.float32)
        weights = (jax.nn.silu(scores) * live[None, None, :] / scale_count).astype(jnp.bfloat16)
        part_sum = jnp.einsum(
            "hck,hkd->chd", weights, value_block, preferred_element_type=jnp.float32
        )
        return accum + part_sum.reshape(rows, local_heads * HEAD_SIZE)

    empty = jnp.zeros((rows, local_heads * HEAD_SIZE), jnp.float32)
    steps = total // block
    if steps == 1:
        return one_block(0, empty)
    return lax.fori_loop(0, steps, one_block, empty)


def finish(attended, gate, norm_gain):
    wide = attended.astype(jnp.float32)
    mean = jnp.mean(wide, axis=1, keepdims=True)
    var = jnp.mean((wide - mean) ** 2, axis=1, keepdims=True)
    normed = (wide - mean) * lax.rsqrt(var + 1e-05) * norm_gain[None, :]
    return (normed * gate.astype(jnp.float32)).astype(jnp.bfloat16)


def per_device(cands, kv_store, proj_weight, norm_gain, users, lengths):
    n_blk = lax.axis_size("blk")
    blk = lax.axis_index("blk")
    slot = lax.axis_index("store")
    ids = jnp.arange(users.shape[0], dtype=jnp.int32)
    chosen = (ids[:, None] == slot) & (users[:, None] == ids[None, :])
    count = jnp.sum(jnp.where(chosen, lengths[None, :], 0))
    half = proj_weight.shape[2]
    local_heads = half // HEAD_SIZE
    n_users, n_pos = (kv_store.shape[0], kv_store.shape[1])
    ordered = (
        kv_store.at[users]
        .get(mode="promise_in_bounds", unique_indices=True)
        .reshape(n_users, n_pos, 2, n_blk, local_heads, HEAD_SIZE)
    )
    ordered = jnp.transpose(ordered, (3, 0, 2, 4, 1, 5)).reshape(
        n_blk * n_users, 2, local_heads, n_pos, HEAD_SIZE
    )
    fetched = lax.all_to_all(ordered, ("blk", "store"), split_axis=0, concat_axis=3, tiled=True)
    keys = fetched[0, 0]
    values = fetched[0, 1]
    mine = cands[0]
    rows = mine.shape[0]

    def project(feats):
        proj = jnp.einsum("cd,dkh->kch", feats, proj_weight, preferred_element_type=jnp.float32)
        query = proj[0].astype(jnp.bfloat16).reshape(-1, local_heads, HEAD_SIZE)
        gate = jax.nn.silu(proj[1]).astype(jnp.bfloat16)
        return (jnp.transpose(query, (1, 0, 2)), gate)

    if n_blk == 2:
        swap = [(0, 1), (1, 0)]
        peer = lax.ppermute(mine, "blk", swap)
        query_own, gate_own = project(mine)
        query_peer, gate_peer = project(peer)
        gate_back = lax.ppermute(gate_peer, "blk", swap)
        row_major = Layout(major_to_minor=(0, 1))
        sent = attend(query_peer, keys, values, count).astype(jnp.bfloat16)
        sent = with_layout_constraint(sent, row_major)
        back = lax.ppermute(sent, "blk", swap)
        query_own, gate_own, _ = lax.optimization_barrier((query_own, gate_own, sent))
        kept = attend(query_own, keys, values, count).astype(jnp.bfloat16)
        kept = with_layout_constraint(kept, row_major)
        first = blk == 0
        attended = jnp.where(
            first, jnp.concatenate([kept, back], axis=1), jnp.concatenate([back, kept], axis=1)
        )
        gate_full = jnp.where(
            first,
            jnp.concatenate([gate_own, gate_back], axis=1),
            jnp.concatenate([gate_back, gate_own], axis=1),
        )
        return finish(attended, gate_full, norm_gain)[None]
    feats = lax.all_gather(mine, "blk", axis=0, tiled=True)
    query, gate = project(feats)
    attended = attend(query, keys, values, count).astype(jnp.bfloat16)
    both = jnp.stack([attended, gate]).reshape(2, n_blk, rows, half)
    own = lax.all_to_all(both, "blk", split_axis=1, concat_axis=3, tiled=True)
    own = own.reshape(2, rows, n_blk * half)
    return finish(own[0], own[1], norm_gain)[None]


def solution(mesh):
    in_specs = (
        P(("batch", "store"), "blk", None),
        P("batch", ("blk", "store"), None, None),
        P(None, None, "blk"),
        P(),
        P("batch"),
        P("batch"),
    )
    out_specs = P(("batch", "store"), "blk", None)
    return jax.shard_map(
        per_device, mesh=mesh, in_specs=in_specs, out_specs=out_specs, check_vma=False
    )
```

profile of v0, /device:TPU:0, one launch (start us, length us, event | category | flops | bytes accessed | tf_op | source)
XLA Modules:
  0.0 37.3 jit_solution(15497531011760025280)
XLA Ops:
  0.0 3.0 %collective-permute-start = (bf16[128,1024]{1,0:T(8,128)(2,1)}, bf16[128,1024]{1,0:T(8,128)(2,1)}, u32[]{:S(2)}, u32[]{:S(2)}) collective-permute-start(bf16[128,1024]{1,0:T(8,128)(2,1)} %bitcast.66), channel_id=1, source_target_pairs={{0,4},{4,0},{1,5},{5,1},{2,6},{6,2},{3,7},{7,3},{8,12},{12,8},{9,1... | collective-permute-start | bytes 786440 | tf_op jit(solution)/shard_map/ppermute | solution.py:81
  3.0 0.7 %compare_select_fusion = s32[4]{0:T(128)S(1)} fusion(s32[4]{0:T(128)} %param.10), kind=kLoop, calls=%fused_computation.42 | loop fusion | flops 12 | bytes 32 | tf_op jit(solution)/shard_map/select_n | solution.py:61
  3.6 2.7 %gather_fusion = bf16[4,64,2,1024]{3,2,1,0:T(2,128)(2,1)S(1)} fusion(bf16[4,64,2,1024]{3,2,1,0:T(2,128)(2,1)S(1)} %copy-done, s32[1024]{0:T(1024)S(1)} %pad_clamp_fusion), kind=kCustom, calls=%fused_computation | custom fusion | bytes 2097168 | tf_op jit(solution)/shard_map/gather | solution.py:61
  6.3 0.7 %reshape.231 = bf16[4,64,2,2,4,128]{5,4,3,2,1,0:T(4,128)(2,1)S(1)} reshape(bf16[4,64,2,1024]{3,2,1,0:T(2,128)(2,1)S(1)} %gather_fusion) | data formatting | bytes 2097152 | tf_op jit(solution)/shard_map/reshape | solution.py:62
  7.0 1.3 %copy.26 = bf16[4,64,2,2,4,128]{5,1,4,2,0,3:T(8,128)(2,1)} copy(bf16[4,64,2,2,4,128]{5,4,3,2,1,0:T(4,128)(2,1)S(1)} %reshape.231) | data formatting | bytes 2097152 | tf_op jit(solution)/shard_map/reshape | solution.py:62
  8.3 4.2 %all-to-all-start = ((bf16[8,2,4,64,128]{4,3,2,1,0:T(8,128)(2,1)}), bf16[8,2,4,64,128]{4,3,2,1,0:T(8,128)(2,1)}, u32[]{:S(2)}, u32[]{:S(2)}) async-start(bf16[8,2,4,64,128]{4,3,2,1,0:T(8,128)(2,1)} %bitcast.1), calls=%async_computation | async-start | bytes 2097152 | tf_op jit(solution)/shard_map/all_to_all | solution.py:67
  12.6 0.0 copy-start.2
  12.6 4.8 %copy.28 = bf16[1024,2,512]{0,2,1:T(8,128)(2,1)S(1)} copy(bf16[1024,2,512]{2,1,0:T(2,128)(2,1)} %param.8) | data formatting | bytes 4194304 | tf_op args[2]
  17.4 0.0 copy-start.4
  17.4 0.0 copy-start.5
  17.4 1.6 %convolution_bitcast_fusion.1 = f32[2,128,512]{2,1,0:T(8,128)} fusion(bf16[1024,2,512]{0,2,1:T(8,128)(2,1)S(1)} %copy.28, bf16[1,128,1024]{2,1,0:T(8,128)(2,1)S(1)} %copy-done.2), kind=kOutput, calls=%fused_computation.4 | convolution fusion | flops 268435456 | bytes 2883584 | tf_op jit(solution)/shard_map/cd,dkh->kch/dot_general | solution.py:74
  19.0 0.7 %select_reduce_fusion = s32[]{:T(128)} fusion(s32[4]{0:T(128)S(1)} %copy-done.4, s32[4]{0:T(128)S(1)} %copy-done.5, pred[4]{0:T(512)(128)(4,1)S(1)} %iota_compare_fusion.2), kind=kLoop, calls=%fused_computation.43 | loop fusion | flops 63 | bytes 40 | tf_op jit(solution)/shard_map/reduce_sum | solution.py:55
  19.8 0.6 %fusion.17 = f32[512]{0:T(512)S(1)} fusion(s32[]{:T(128)} %select_reduce_fusion), kind=kLoop, calls=%fused_computation.46 | loop fusion | flops 1024 | bytes 2052 | tf_op jit(solution)/shard_map/convert_element_type | solution.py:27
  21.1 1.0 %slice.51 = bf16[1,128,512]{2,1,0:T(8,128)(2,1)S(1)} slice(f32[2,128,512]{2,1,0:T(8,128)} %convolution_bitcast_fusion.1), slice={[0:1], [0:128], [0:512]} | slice | bytes 262144 | tf_op jit(solution)/shard_map/slice | solution.py:75
  22.1 1.0 %multiply_convert_fusion.2 = bf16[128,512]{1,0:T(8,128)(2,1)S(1)} fusion(f32[2,128,512]{2,1,0:T(8,128)} %convolution_bitcast_fusion.1), kind=kLoop, calls=%fused_computation.35 | loop fusion | flops 327680 | bytes 393216 | tf_op jit(solution)/shard_map/convert_element_type | solution.py:76
  23.1 0.0 collective-permute-done
  23.1 1.8 %convolution_bitcast_fusion = f32[2,128,512]{2,1,0:T(8,128)S(1)} fusion(bf16[1024,2,512]{0,2,1:T(8,128)(2,1)S(1)} %copy.28, bf16[128,1024]{1,0:T(8,128)(2,1)} %collective-permute-done), kind=kOutput, calls=%fused_computation.3 | convolution fusion | flops 268435456 | bytes 2883584 | tf_op jit(solution)/shard_map/cd,dkh->kch/dot_general | solution.py:74
  24.9 0.8 %copy-done.1 = f32[2,128,512]{2,1,0:T(8,128)} copy-done((f32[2,128,512]{2,1,0:T(8,128)}, f32[2,128,512]{2,1,0:T(8,128)S(1)}, u32[]{:S(2)}) %copy-start.1) | copy-done | bytes 524312
  25.8 1.0 %multiply_convert_fusion.1 = bf16[128,512]{1,0:T(8,128)(2,1)S(1)} fusion(f32[2,128,512]{2,1,0:T(8,128)} %copy-done.1), kind=kLoop, calls=%fused_computation.34 | loop fusion | flops 327680 | bytes 393216 | tf_op jit(solution)/shard_map/convert_element_type | solution.py:76
  26.8 2.0 %collective-permute-start.2 = (bf16[128,512]{1,0:T(8,128)(2,1)S(1)}, bf16[128,512]{1,0:T(8,128)(2,1)S(1)}, u32[]{:S(2)}, u32[]{:S(2)}) collective-permute-start(bf16[128,512]{1,0:T(8,128)(2,1)S(1)} %multiply_convert_fusion.1), channel_id=1, source_target_pairs={{0,4},{4,0},{1,5},{5,1},{2,6},{6,2},{3,7},{7,3},{8,12},{12,8},{9,1... | collective-permute-start | bytes 393224 | tf_op jit(solution)/shard_map/ppermute | solution.py:84
  28.8 0.0 all-to-all-done
  28.8 1.3 %copy.27 = bf16[1,2,4,8,64,128]{5,4,3,2,1,0:T(8,128)(2,1)S(1)} copy(bf16[1,2,4,8,64,128]{5,4,2,1,3,0:T(8,128)(2,1)} %bitcast.3) | data formatting | bytes 2097152 | tf_op jit(solution)/shard_map/all_to_all | solution.py:67
  30.1 0.6 %fusion = bf16[4,16,8,128]{3,2,1,0:T(8,128)(2,1)S(1)} fusion(f32[]{:T(128)S(6)} %convert_element_type.88, f32[512]{0:T(512)S(1)} %fusion.17, bf16[1,2,4,512,128]{4,3,2,1,0:T(8,128)(2,1)S(1)} %bitcast.62, bf16[128,4,128]{2,1,0:T(4,128)(2,1)S(1)} %convert_element_type.86), kind=kOutput, calls=%fused_computation.7 | convolution fusion | flops 136380416 | bytes 1312772 | tf_op jit(solution)/shard_map/hck,hkd->chd/dot_general | solution.py:29
  30.8 0.2 collective-permute-start.1
  31.0 0.6 %convolution_convert_fusion = bf16[4,128,128]{1,2,0:T(8,128)(2,1)S(1)} fusion(bf16[4,128,128]{2,1,0:T(8,128)(2,1)S(1)} %bitcast.67, f32[]{:T(128)S(6)} %convert_element_type.88, f32[512]{0:T(512)S(1)} %fusion.17, bf16[1,2,4,512,128]{4,3,2,1,0:T(8,128)(2,1)S(1)} %bitcast.63), kind=kOutput, calls=%fused_computation.5 | convolution fusion | flops 136380416 | bytes 1312772 | tf_op jit(solution)/shard_map/hck,hkd->chd/dot_general | solution.py:29
  31.6 0.1 copy.35
  31.7 0.1 concatenate.52
  31.8 4.3 %collective-permute-done.1 = bf16[128,512]{1,0:T(8,128)(2,1)S(1)} collective-permute-done((bf16[128,512]{1,0:T(8,128)(2,1)S(1)}, bf16[128,512]{1,0:T(8,128)(2,1)S(1)}, u32[]{:S(2)}, u32[]{:S(2)}) %collective-permute-start.1) | collective-permute-done | bytes 131104 | tf_op jit(solution)/shard_map/ppermute | solution.py:88
  36.1 0.1 convert_reduce_fusion
  36.2 0.2 fusion.2
  36.5 0.0 collective-permute-done.2
  36.5 0.9 %multiply_convert_fusion = bf16[1,128,1024]{2,1,0:T(8,128)(2,1)} fusion(bf16[1,128,512]{2,1,0:T(8,128)(2,1)S(1)} %bitcast.61, bf16[1,128,512]{2,1,0:T(8,128)(2,1)S(1)} %concatenate.52, bf16[1,128,512]{2,1,0:T(8,128)(2,1)S(1)} %bitcast.69, bf16[1,128,512]{2,1,0:T(8,128)(2,1)S(1)} %bitcast.64, f32[1024]{0:T(1024)S(1)} %copy-done.3, f32[128]{0:T(128)S(1)} %add_rsqrt_fusion, ...), kind=kLoop, calls=%fused_computation.16 | loop fusion | flops 3276800 | bytes 791553 | tf_op jit(solution)/shard_map/convert_element_type | solution.py:46
  (18 shorter events, 0.2 us)
Async XLA Ops:
  0.0 3.6 %copy-start = (bf16[4,64,2,1024]{3,2,1,0:T(2,128)(2,1)S(1)}, bf16[4,64,2,1024]{3,2,1,0:T(2,128)(2,1)}, u32[]{:S(2)}) copy-start(bf16[4,64,2,1024]{3,2,1,0:T(2,128)(2,1)} %param.7) | copy-start | bytes 3145732
  0.0 23.1 %collective-permute-start = (bf16[128,1024]{1,0:T(8,128)(2,1)}, bf16[128,1024]{1,0:T(8,128)(2,1)}, u32[]{:S(2)}, u32[]{:S(2)}) collective-permute-start(bf16[128,1024]{1,0:T(8,128)(2,1)} %bitcast.66), channel_id=1, source_target_pairs={{0,4},{4,0},{1,5},{5,1},{2,6},{6,2},{3,7},{7,3},{8,12},{12,8},{9,1... | collective-permute-start | bytes 786440 | tf_op jit(solution)/shard_map/ppermute | solution.py:81
  8.3 20.4 %all-to-all-start = ((bf16[8,2,4,64,128]{4,3,2,1,0:T(8,128)(2,1)}), bf16[8,2,4,64,128]{4,3,2,1,0:T(8,128)(2,1)}, u32[]{:S(2)}, u32[]{:S(2)}) async-start(bf16[8,2,4,64,128]{4,3,2,1,0:T(8,128)(2,1)} %bitcast.1), calls=%async_computation | async-start | bytes 2097152 | tf_op jit(solution)/shard_map/all_to_all | solution.py:67
  12.6 4.8 %copy-start.2 = (bf16[1,128,1024]{2,1,0:T(8,128)(2,1)S(1)}, bf16[1,128,1024]{2,1,0:T(8,128)(2,1)}, u32[]{:S(2)}) copy-start(bf16[1,128,1024]{2,1,0:T(8,128)(2,1)} %param.6) | copy-start | bytes 786436
  17.4 1.6 %copy-start.4 = (s32[4]{0:T(128)S(1)}, s32[4]{0:T(128)}, u32[]{:S(2)}) copy-start(s32[4]{0:T(128)} %param.11) | copy-start | bytes 52
  17.4 1.6 %copy-start.5 = (s32[4]{0:T(128)S(1)}, s32[4]{0:T(128)}, u32[]{:S(2)}) copy-start(s32[4]{0:T(128)} %param.10) | copy-start | bytes 52
  24.9 0.8 %copy-start.1 = (f32[2,128,512]{2,1,0:T(8,128)}, f32[2,128,512]{2,1,0:T(8,128)S(1)}, u32[]{:S(2)}) copy-start(f32[2,128,512]{2,1,0:T(8,128)S(1)} %convolution_bitcast_fusion) | copy-start | bytes 1572868
  26.8 9.6 %collective-permute-start.2 = (bf16[128,512]{1,0:T(8,128)(2,1)S(1)}, bf16[128,512]{1,0:T(8,128)(2,1)S(1)}, u32[]{:S(2)}, u32[]{:S(2)}) collective-permute-start(bf16[128,512]{1,0:T(8,128)(2,1)S(1)} %multiply_convert_fusion.1), channel_id=1, source_target_pairs={{0,4},{4,0},{1,5},{5,1},{2,6},{6,2},{3,7},{7,3},{8,12},{12,8},{9,1... | collective-permute-start | bytes 393224 | tf_op jit(solution)/shard_map/ppermute | solution.py:84
  30.8 5.3 %collective-permute-start.1 = (bf16[128,512]{1,0:T(8,128)(2,1)S(1)}, bf16[128,512]{1,0:T(8,128)(2,1)S(1)}, u32[]{:S(2)}, u32[]{:S(2)}) collective-permute-start(bf16[128,512]{1,0:T(8,128)(2,1)S(1)} %bitcast.68), channel_id=1, source_target_pairs={{0,4},{4,0},{1,5},{5,1},{2,6},{6,2},{3,7},{7,3},{8,12},{12,8},{9,1... | collective-permute-start | bytes 393224 | tf_op jit(solution)/shard_map/ppermute | solution.py:88
  31.0 5.5 %copy-start.3 = (f32[1024]{0:T(1024)S(1)}, f32[1024]{0:T(1024)}, u32[]{:S(2)}) copy-start(f32[1024]{0:T(1024)} %param.9) | copy-start | bytes 12292
where the time goes:
time: 37.8 us; the launch traced here: 37.3 us
  local copies, waits for them, and re-layouts  12.8 us (34%)
  starting transfers between devices  9.38 us (25%)
  other arithmetic  5.31 us (14%)
  matrix products  4.67 us (12%)
  waiting for transfers between devices  4.29 us (11%)
  between operations  0.85 us (2%)
    unnamed x13, local copies, waits for them, and re-layouts  5.58 us
    ppermute x1, waiting for transfers between devices, per_device(): back = lax.ppermute(sent, 'blk', swap)  4.29 us
    all_to_all x1, starting transfers between devices, per_device(): lax.all_to_all(ordered, ('blk', 'store'), split_axis=0, concat_axis=3, ti...  4.24 us
    dot_general x2, matrix products, project(): jnp.einsum('cd,dkh->kch', feats, proj_weight, preferred_element_type=jnp....  3.4 us
    ppermute x1, starting transfers between devices, per_device(): peer = lax.ppermute(mine, 'blk', swap)  2.97 us
    gather x1, local copies, waits for them, and re-layouts, per_device(): ordered = kv_store.at[users].get(mode='promise_in_bounds', unique_indices...  2.66 us
    convert_element_type x2, other arithmetic, project(): gate = jax.nn.silu(proj[1]).astype(jnp.bfloat16)  2.06 us
    reshape x2, local copies, waits for them, and re-layouts, per_device(): ordered = kv_store.at[users].get(mode='promise_in_bounds', unique_indices...  2.02 us
  transfers between devices with their start and end apart: 4, of which 1 were waited for; matrix products, arithmetic and copies ran while one was open for 57% of the time, Pallas kernels for 0%

commit v1 on v0

--- a/solution.py
+++ b/solution.py
@@ -1,3 +1,4 @@
+import functools
 import jax
 import jax.numpy as jnp
 from jax import lax
@@ -7,6 +8,17 @@
 D = 1024
 HEADS = 8
 HEAD_SIZE = D // HEADS
+
+
+def test_area(w_in, bus_axis):
+    b_now = jax.lax.psum(1, bus_axis)
+    then = jnp.split(w_in, b_now, axis=0)
+    mid_arr = jnp.stack(then)
+    left_arr = jax.lax.all_to_all(mid_arr, bus_axis, 0, 0)
+    return jnp.concatenate(left_arr, axis=3)
+
+
+_wait_panel = functools.partial(test_area, bus_axis=("blk", "store"))
 
 
 def attend(qheads, keys, values, count):
@@ -64,7 +76,7 @@
     ordered = jnp.transpose(ordered, (3, 0, 2, 4, 1, 5)).reshape(
         n_blk * n_users, 2, local_heads, n_pos, HEAD_SIZE
     )
-    fetched = lax.all_to_all(ordered, ("blk", "store"), split_axis=0, concat_axis=3, tiled=True)
+    fetched = _wait_panel(ordered)
     keys = fetched[0, 0]
     values = fetched[0, 1]
     mine = cands[0]

time: 37.8 us -> 42 us (1.11)
  local copies, waits for them, and re-layouts: 12.8 us -> 17.1 us
    unnamed x13 -> x20, local copies, waits for them, and re-layouts: 5.58 us -> 10.2 us
    all_to_all x1 -> x0, local copies, waits for them, and re-layouts: 1.31 us -> none  [per_device(): lax.all_to_all(ordered, ('blk', 'store'), split_axis=0, concat_axis=3, ti...]
    reshape x0 -> x1, local copies, waits for them, and re-layouts: none -> 1.31 us  [test_area(): return jnp.concatenate(left_arr, axis=3)]
    reshape x2, local copies, waits for them, and re-layouts: 2.02 us -> 0.98 us  [per_device(): ordered = kv_store.at[users].get(mode='promise_in_bounds', unique_indices...]
    another operation x0 -> x1, local copies, waits for them, and re-layouts: none -> 0.65 us  [test_area(): mid_arr = jnp.stack(then)]
  transfers between devices with their start and end apart: 4 -> 4, of which waited for: 1 -> 1; matrix products, arithmetic and copies ran while one was open for 57% -> 61% of each run, Pallas kernels for 0% -> 0%
where the time goes in v1:
time: 42 us; the launch traced here: 41.6 us
  local copies, waits for them, and re-layouts  17.1 us (41%)
  starting transfers between devices  9.38 us (22%)
  other arithmetic  5.31 us (13%)
  matrix products  4.67 us (11%)
  waiting for transfers between devices  4.29 us (10%)
  between operations  0.87 us (2%)
    unnamed x20, local copies, waits for them, and re-layouts  10.2 us
    ppermute x1, waiting for transfers between devices, per_device(): back = lax.ppermute(sent, 'blk', swap)  4.29 us
    all_to_all x1, starting transfers between devices, test_area(): left_arr = jax.lax.all_to_all(mid_arr, bus_axis, 0, 0)  4.24 us
    dot_general x2, matrix products, project(): jnp.einsum('cd,dkh->kch', feats, proj_weight, preferred_element_type=jnp....  3.39 us
    ppermute x1, starting transfers between devices, per_device(): peer = lax.ppermute(mine, 'blk', swap)  2.97 us
    gather x1, local copies, waits for them, and re-layouts, per_device(): ordered = kv_store.at[users].get(mode='promise_in_bounds', unique_indices...  2.66 us
    convert_element_type x2, other arithmetic, project(): gate = jax.nn.silu(proj[1]).astype(jnp.bfloat16)  2.06 us
    ppermute x1, starting transfers between devices, per_device(): gate_back = lax.ppermute(gate_peer, 'blk', swap)  1.96 us
  transfers between devices with their start and end apart: 4, of which 1 were waited for; matrix products, arithmetic and copies ran while one was open for 61% of the time, Pallas kernels for 0%

profile of v1, /device:TPU:0, one launch (start us, length us, event | category | flops | bytes accessed | tf_op | source)
XLA Modules:
  0.0 41.6 jit_solution(1324373473761873469)
XLA Ops:
  0.0 3.0 %collective-permute-start = (bf16[128,1024]{1,0:T(8,128)(2,1)}, bf16[128,1024]{1,0:T(8,128)(2,1)}, u32[]{:S(2)}, u32[]{:S(2)}) collective-permute-start(bf16[128,1024]{1,0:T(8,128)(2,1)} %bitcast.104), channel_id=1, source_target_pairs={{0,4},{4,0},{1,5},{5,1},{2,6},{6,2},{3,7},{7,3},{8,12},{12,8},{9,1... | collective-permute-start | bytes 786440 | tf_op jit(solution)/shard_map/ppermute | solution.py:93
  3.0 0.7 %compare_select_fusion = s32[4]{0:T(128)S(1)} fusion(s32[4]{0:T(128)} %param.10), kind=kLoop, calls=%fused_computation.58 | loop fusion | flops 12 | bytes 32 | tf_op jit(solution)/shard_map/select_n | solution.py:73
  3.6 2.7 %gather_fusion = bf16[4,64,2,1024]{3,2,1,0:T(2,128)(2,1)S(1)} fusion(bf16[4,64,2,1024]{3,2,1,0:T(2,128)(2,1)S(1)} %copy-done, s32[1024]{0:T(1024)S(1)} %pad_clamp_fusion), kind=kCustom, calls=%fused_computation | custom fusion | bytes 2097168 | tf_op jit(solution)/shard_map/gather | solution.py:73
  6.3 0.7 %reshape.237 = bf16[4,64,2,2,4,128]{5,4,3,2,1,0:T(4,128)(2,1)S(1)} reshape(bf16[4,64,2,1024]{3,2,1,0:T(2,128)(2,1)S(1)} %gather_fusion) | data formatting | bytes 2097152 | tf_op jit(solution)/shard_map/reshape | solution.py:74
  7.0 0.3 copy.33
  7.3 0.7 %fusion.20 = bf16[8,1,2,4,64,128]{5,4,3,2,1,0:T(8,128)(2,1)} fusion(bf16[8,2,4,64,128]{4,3,2,1,0:T(8,128)(2,1)S(1)} %bitcast.91), kind=kLoop, calls=%fused_computation.53 | loop fusion | bytes 262144
  8.0 0.7 %fusion.19 = bf16[8,1,2,4,64,128]{5,4,3,2,1,0:T(8,128)(2,1)} fusion(bf16[8,1,2,4,64,128]{5,4,3,2,1,0:T(8,128)(2,1)} %fusion.20, bf16[8,2,4,64,128]{4,3,2,1,0:T(8,128)(2,1)S(1)} %bitcast.92), kind=kLoop, calls=%fused_computation.51 | loop fusion | bytes 262144
  8.6 0.7 %fusion.18 = bf16[8,1,2,4,64,128]{5,4,3,2,1,0:T(8,128)(2,1)} fusion(bf16[8,1,2,4,64,128]{5,4,3,2,1,0:T(8,128)(2,1)} %fusion.19, bf16[8,2,4,64,128]{4,3,2,1,0:T(8,128)(2,1)S(1)} %bitcast.93), kind=kLoop, calls=%fused_computation.49 | loop fusion | bytes 262144
  9.3 0.6 %fusion.17 = bf16[8,1,2,4,64,128]{5,4,3,2,1,0:T(8,128)(2,1)} fusion(bf16[8,1,2,4,64,128]{5,4,3,2,1,0:T(8,128)(2,1)} %fusion.18, bf16[8,2,4,64,128]{4,3,2,1,0:T(8,128)(2,1)S(1)} %bitcast.94), kind=kLoop, calls=%fused_computation.47 | loop fusion | bytes 262144
  9.9 0.7 %fusion.16 = bf16[8,1,2,4,64,128]{5,4,3,2,1,0:T(8,128)(2,1)} fusion(bf16[8,1,2,4,64,128]{5,4,3,2,1,0:T(8,128)(2,1)} %fusion.17, bf16[8,2,4,64,128]{4,3,2,1,0:T(8,128)(2,1)S(1)} %bitcast.95), kind=kLoop, calls=%fused_computation.45 | loop fusion | bytes 262144
  10.6 0.7 %fusion.15 = bf16[8,1,2,4,64,128]{5,4,3,2,1,0:T(8,128)(2,1)} fusion(bf16[8,1,2,4,64,128]{5,4,3,2,1,0:T(8,128)(2,1)} %fusion.16, bf16[8,2,4,64,128]{4,3,2,1,0:T(8,128)(2,1)S(1)} %bitcast.96), kind=kLoop, calls=%fused_computation.43 | loop fusion | bytes 262144
  11.3 0.7 %fusion.14 = bf16[8,1,2,4,64,128]{5,4,3,2,1,0:T(8,128)(2,1)} fusion(bf16[8,1,2,4,64,128]{5,4,3,2,1,0:T(8,128)(2,1)} %fusion.15, bf16[8,2,4,64,128]{4,3,2,1,0:T(8,128)(2,1)S(1)} %bitcast.97), kind=kLoop, calls=%fused_computation.41 | loop fusion | bytes 262144
  11.9 0.7 %fusion.13 = bf16[8,1,2,4,64,128]{5,4,3,2,1,0:T(8,128)(2,1)} fusion(bf16[8,1,2,4,64,128]{5,4,3,2,1,0:T(8,128)(2,1)} %fusion.14, bf16[8,2,4,64,128]{4,3,2,1,0:T(8,128)(2,1)S(1)} %bitcast.98), kind=kLoop, calls=%fused_computation.39 | loop fusion | bytes 262144 | tf_op jit(solution)/shard_map/stack | solution.py:16
  12.6 4.2 %all-to-all-start = ((bf16[8,1,2,4,64,128]{5,4,3,2,1,0:T(8,128)(2,1)}), bf16[8,1,2,4,64,128]{5,4,3,2,1,0:T(8,128)(2,1)}, u32[]{:S(2)}, u32[]{:S(2)}) async-start(bf16[8,1,2,4,64,128]{5,4,3,2,1,0:T(8,128)(2,1)} %fusion.13), calls=%async_computation | async-start | bytes 2097152 | tf_op jit(solution)/shard_map/all_to_all | solution.py:17
  16.9 4.8 %copy.35 = bf16[1024,2,512]{0,2,1:T(8,128)(2,1)S(1)} copy(bf16[1024,2,512]{2,1,0:T(2,128)(2,1)} %param.8) | data formatting | bytes 4194304 | tf_op args[2]
  21.7 1.6 %convolution_bitcast_fusion.1 = f32[2,128,512]{2,1,0:T(8,128)} fusion(bf16[1024,2,512]{0,2,1:T(8,128)(2,1)S(1)} %copy.35, bf16[1,128,1024]{2,1,0:T(8,128)(2,1)S(1)} %copy-done.2), kind=kOutput, calls=%fused_computation.4 | convolution fusion | flops 268435456 | bytes 2883584 | tf_op jit(solution)/shard_map/cd,dkh->kch/dot_general | solution.py:86
  23.3 0.7 %select_reduce_fusion = s32[]{:T(128)} fusion(s32[4]{0:T(128)S(1)} %copy-done.4, s32[4]{0:T(128)S(1)} %copy-done.5, pred[4]{0:T(512)(128)(4,1)S(1)} %iota_compare_fusion.2), kind=kLoop, calls=%fused_computation.59 | loop fusion | flops 63 | bytes 40 | tf_op jit(solution)/shard_map/reduce_sum | solution.py:67
  24.0 0.6 %fusion.25 = f32[512]{0:T(512)S(1)} fusion(s32[]{:T(128)} %select_reduce_fusion), kind=kLoop, calls=%fused_computation.62 | loop fusion | flops 1024 | bytes 2052 | tf_op jit(solution)/shard_map/convert_element_type | solution.py:39
  25.3 1.0 %slice.51 = bf16[1,128,512]{2,1,0:T(8,128)(2,1)S(1)} slice(f32[2,128,512]{2,1,0:T(8,128)} %convolution_bitcast_fusion.1), slice={[0:1], [0:128], [0:512]} | slice | bytes 262144 | tf_op jit(solution)/shard_map/slice | solution.py:87
  26.4 1.0 %multiply_convert_fusion.2 = bf16[128,512]{1,0:T(8,128)(2,1)S(1)} fusion(f32[2,128,512]{2,1,0:T(8,128)} %convolution_bitcast_fusion.1), kind=kLoop, calls=%fused_computation.35 | loop fusion | flops 327680 | bytes 393216 | tf_op jit(solution)/shard_map/convert_element_type | solution.py:88
  27.4 1.8 %convolution_bitcast_fusion = f32[2,128,512]{2,1,0:T(8,128)S(1)} fusion(bf16[1024,2,512]{0,2,1:T(8,128)(2,1)S(1)} %copy.35, bf16[128,1024]{1,0:T(8,128)(2,1)} %collective-permute-done), kind=kOutput, calls=%fused_computation.3 | convolution fusion | flops 268435456 | bytes 2883584 | tf_op jit(solution)/shard_map/cd,dkh->kch/dot_general | solution.py:86
  29.2 0.8 %copy-done.1 = f32[2,128,512]{2,1,0:T(8,128)} copy-done((f32[2,128,512]{2,1,0:T(8,128)}, f32[2,128,512]{2,1,0:T(8,128)S(1)}, u32[]{:S(2)}) %copy-start.1) | copy-done | bytes 524312
  30.0 1.0 %multiply_convert_fusion.1 = bf16[128,512]{1,0:T(8,128)(2,1)S(1)} fusion(f32[2,128,512]{2,1,0:T(8,128)} %copy-done.1), kind=kLoop, calls=%fused_computation.34 | loop fusion | flops 327680 | bytes 393216 | tf_op jit(solution)/shard_map/convert_element_type | solution.py:88
  31.1 2.0 %collective-permute-start.2 = (bf16[128,512]{1,0:T(8,128)(2,1)S(1)}, bf16[128,512]{1,0:T(8,128)(2,1)S(1)}, u32[]{:S(2)}, u32[]{:S(2)}) collective-permute-start(bf16[128,512]{1,0:T(8,128)(2,1)S(1)} %multiply_convert_fusion.1), channel_id=1, source_target_pairs={{0,4},{4,0},{1,5},{5,1},{2,6},{6,2},{3,7},{7,3},{8,12},{12,8},{9,1... | collective-permute-start | bytes 393224 | tf_op jit(solution)/shard_map/ppermute | solution.py:96
  33.0 1.3 %copy.34 = bf16[1,2,4,8,64,128]{5,4,3,2,1,0:T(8,128)(2,1)S(1)} copy(bf16[1,2,4,8,64,128]{5,4,2,1,0,3:T(8,128)(2,1)} %bitcast.11) | data formatting | bytes 2097152 | tf_op jit(solution)/shard_map/reshape | solution.py:18
  34.3 0.6 %fusion = bf16[4,16,8,128]{3,2,1,0:T(8,128)(2,1)S(1)} fusion(f32[]{:T(128)S(6)} %convert_element_type.88, f32[512]{0:T(512)S(1)} %fusion.25, bf16[1,2,4,512,128]{4,3,2,1,0:T(8,128)(2,1)S(1)} %bitcast.100, bf16[128,4,128]{2,1,0:T(4,128)(2,1)S(1)} %convert_element_type.86), kind=kOutput, calls=%fused_computation.7 | convolution fusion | flops 136380416 | bytes 1312772 | tf_op jit(solution)/shard_map/hck,hkd->chd/dot_general | solution.py:41
  35.0 0.2 collective-permute-start.1
  35.2 0.6 %convolution_convert_fusion = bf16[4,128,128]{1,2,0:T(8,128)(2,1)S(1)} fusion(bf16[4,128,128]{2,1,0:T(8,128)(2,1)S(1)} %bitcast.105, f32[]{:T(128)S(6)} %convert_element_type.88, f32[512]{0:T(512)S(1)} %fusion.25, bf16[1,2,4,512,128]{4,3,2,1,0:T(8,128)(2,1)S(1)} %bitcast.101), kind=kOutput, calls=%fused_computation.5 | convolution fusion | flops 136380416 | bytes 1312772 | tf_op jit(solution)/shard_map/hck,hkd->chd/dot_general | solution.py:41
  36.1 4.3 %collective-permute-done.1 = bf16[128,512]{1,0:T(8,128)(2,1)S(1)} collective-permute-done((bf16[128,512]{1,0:T(8,128)(2,1)S(1)}, bf16[128,512]{1,0:T(8,128)(2,1)S(1)}, u32[]{:S(2)}, u32[]{:S(2)}) %collective-permute-start.1) | collective-permute-done | bytes 131104 | tf_op jit(solution)/shard_map/ppermute | solution.py:100
  40.4 0.1 convert_reduce_fusion
  40.5 0.2 fusion.2
  40.7 0.9 %multiply_convert_fusion = bf16[1,128,1024]{2,1,0:T(8,128)(2,1)} fusion(bf16[1,128,512]{2,1,0:T(8,128)(2,1)S(1)} %bitcast.99, bf16[1,128,512]{2,1,0:T(8,128)(2,1)S(1)} %concatenate.52, bf16[1,128,512]{2,1,0:T(8,128)(2,1)S(1)} %bitcast.107, bf16[1,128,512]{2,1,0:T(8,128)(2,1)S(1)} %bitcast.102, f32[1024]{0:T(1024)S(1)} %copy-done.3, ...), kind=kLoop, calls=%fused_computation.16 | loop fusion | flops 3276800 | bytes 791553 | tf_op jit(solution)/shard_map/convert_element_type | solution.py:58
  (26 shorter events, 0.4 us)
Async XLA Ops:
  0.0 3.6 %copy-start = (bf16[4,64,2,1024]{3,2,1,0:T(2,128)(2,1)S(1)}, bf16[4,64,2,1024]{3,2,1,0:T(2,128)(2,1)}, u32[]{:S(2)}) copy-start(bf16[4,64,2,1024]{3,2,1,0:T(2,128)(2,1)} %param.7) | copy-start | bytes 3145732
  0.0 27.4 %collective-permute-start = (bf16[128,1024]{1,0:T(8,128)(2,1)}, bf16[128,1024]{1,0:T(8,128)(2,1)}, u32[]{:S(2)}, u32[]{:S(2)}) collective-permute-start(bf16[128,1024]{1,0:T(8,128)(2,1)} %bitcast.104), channel_id=1, source_target_pairs={{0,4},{4,0},{1,5},{5,1},{2,6},{6,2},{3,7},{7,3},{8,12},{12,8},{9,1... | collective-permute-start | bytes 786440 | tf_op jit(solution)/shard_map/ppermute | solution.py:93
  12.6 20.4 %all-to-all-start = ((bf16[8,1,2,4,64,128]{5,4,3,2,1,0:T(8,128)(2,1)}), bf16[8,1,2,4,64,128]{5,4,3,2,1,0:T(8,128)(2,1)}, u32[]{:S(2)}, u32[]{:S(2)}) async-start(bf16[8,1,2,4,64,128]{5,4,3,2,1,0:T(8,128)(2,1)} %fusion.13), calls=%async_computation | async-start | bytes 2097152 | tf_op jit(solution)/shard_map/all_to_all | solution.py:17
  16.8 4.8 %copy-start.2 = (bf16[1,128,1024]{2,1,0:T(8,128)(2,1)S(1)}, bf16[1,128,1024]{2,1,0:T(8,128)(2,1)}, u32[]{:S(2)}) copy-start(bf16[1,128,1024]{2,1,0:T(8,128)(2,1)} %param.6) | copy-start | bytes 786436
  21.7 1.6 %copy-start.4 = (s32[4]{0:T(128)S(1)}, s32[4]{0:T(128)}, u32[]{:S(2)}) copy-start(s32[4]{0:T(128)} %param.11) | copy-start | bytes 52
  21.7 1.6 %copy-start.5 = (s32[4]{0:T(128)S(1)}, s32[4]{0:T(128)}, u32[]{:S(2)}) copy-start(s32[4]{0:T(128)} %param.10) | copy-start | bytes 52
  29.2 0.8 %copy-start.1 = (f32[2,128,512]{2,1,0:T(8,128)}, f32[2,128,512]{2,1,0:T(8,128)S(1)}, u32[]{:S(2)}) copy-start(f32[2,128,512]{2,1,0:T(8,128)S(1)} %convolution_bitcast_fusion) | copy-start | bytes 1572868
  31.1 9.7 %collective-permute-start.2 = (bf16[128,512]{1,0:T(8,128)(2,1)S(1)}, bf16[128,512]{1,0:T(8,128)(2,1)S(1)}, u32[]{:S(2)}, u32[]{:S(2)}) collective-permute-start(bf16[128,512]{1,0:T(8,128)(2,1)S(1)} %multiply_convert_fusion.1), channel_id=1, source_target_pairs={{0,4},{4,0},{1,5},{5,1},{2,6},{6,2},{3,7},{7,3},{8,12},{12,8},{9,1... | collective-permute-start | bytes 393224 | tf_op jit(solution)/shard_map/ppermute | solution.py:96
  35.0 5.3 %collective-permute-start.1 = (bf16[128,512]{1,0:T(8,128)(2,1)S(1)}, bf16[128,512]{1,0:T(8,128)(2,1)S(1)}, u32[]{:S(2)}, u32[]{:S(2)}) collective-permute-start(bf16[128,512]{1,0:T(8,128)(2,1)S(1)} %bitcast.106), channel_id=1, source_target_pairs={{0,4},{4,0},{1,5},{5,1},{2,6},{6,2},{3,7},{7,3},{8,12},{12,8},{9,1... | collective-permute-start | bytes 393224 | tf_op jit(solution)/shard_map/ppermute | solution.py:100
  35.2 5.5 %copy-start.3 = (f32[1024]{0:T(1024)S(1)}, f32[1024]{0:T(1024)}, u32[]{:S(2)}) copy-start(f32[1024]{0:T(1024)} %param.9) | copy-start | bytes 12292
